TPU v7x, 512 devices: a whole 4x8x8 slice. The times are simulated.
512 devices in a mesh: section: 64 (over y_hi, z, x), rep: 8 (over y_lo, core).
Axes of the slice: x: 4, y: 8 (y_hi: 2, y_lo: 4; y = y_hi * 4 + y_lo), z: 8, core: 2. Of those that a mesh axis runs over, the one named last changes fastest.
Arguments:
- features: bfloat16 [65536, 512], P(('section', 'rep')), may hold values from -6 to 6
- col_panels: int32 [512, 8, 12], P('section', 'rep'), may hold values from 0 to 511, as said below
- block_counts: int32 [512, 8], P('section', 'rep'), may hold values from 1 to 12, as said below
- block_values: bfloat16 [512, 8, 12, 128, 128], P('section', 'rep'), may hold values from 0.0019989014 to 0.019897461
- weight: bfloat16 [512, 512], replicated, may hold values from -0.25 to 0.25
- bias: float32 [512], replicated, may hold values from -3 to 3
- cotangent: bfloat16 [65536, 512], P(('section', 'rep')), may hold values from -6 to 6
Outputs:
- hidden: bfloat16 [65536, 512], P(('section', 'rep'))
- weight_grad: float32 [512, 512], replicated
- bias_grad: float32 [512], replicated
Inputs may be any that keep to these rules, and one draw needn't show every extreme that they name: Column group r holds the column panels c with (c) % 8 == r; col_panels[p, r, k] lies in column group r, and the 12 entries of one list are distinct. Only the first block_counts[p, r] slots of a list are nonzero blocks; later slots are ignored. The count 12 occurs in every draw.
All inputs are finite; a program needn't handle non-finite values.
Results may differ from a plain program's by a relative error of at most 0.0055.
Values may be sent and summed in bfloat16 or wider, within the bound.
No kernel may reach another device: no remote copies, remote signals or barrier semaphores. Data moves between devices by JAX's collectives and lax.ppermute only.
A program may use at most 64 MiB of HBM per device.

v0:
```python
import math
import jax
import jax.numpy as jnp
from jax import lax
from jax.sharding import PartitionSpec as P


def shards(features, col_panels, block_counts, block_values, weight, bias, cotangent):
    rep_count = lax.axis_size("rep")
    rep_index = lax.axis_index("rep")
    tile_size = block_values.shape[-1]
    feat_width = features.shape[1]
    own_panels = features.shape[0] // tile_size
    row_panels = col_panels.shape[0]
    slot_count = col_panels.shape[2]
    global_cols = col_panels[:, 0, :]
    local_cols = global_cols // (own_panels * rep_count) * own_panels + global_cols % own_panels
    live_counts = block_counts[:, 0]
    slot_mask = jnp.arange(slot_count, dtype=jnp.int32)[None, :] < live_counts[:, None]
    tiles = block_values[:, 0]
    empty = jnp.zeros((row_panels, tile_size, feat_width), jnp.float32)
    gathered = lax.all_gather(features, "section", axis=0, tiled=True)
    all_panels = gathered.reshape(-1, tile_size, feat_width)
    slot_step = 4
    turn_count = (jnp.max(live_counts) + slot_step - 1) // slot_step

    def one_turn(turn, running):
        begin_slot = turn * slot_step
        step_cols = lax.dynamic_slice_in_dim(local_cols, begin_slot, slot_step, 1)
        step_mask = lax.dynamic_slice_in_dim(slot_mask, begin_slot, slot_step, 1)
        step_tiles = lax.dynamic_slice_in_dim(tiles, begin_slot, slot_step, 1)
        step_tiles = jnp.where(step_mask[:, :, None, None], step_tiles, jnp.zeros((), jnp.bfloat16))
        picked = all_panels[step_cols]
        return running + jnp.einsum(
            "gkab,gkbf->gaf", step_tiles, picked, preferred_element_type=jnp.float32
        )

    gathered_sum = lax.fori_loop(0, turn_count, one_turn, empty)
    partial_value = gathered_sum.reshape(row_panels * tile_size, feat_width)
    own_rows = own_panels * tile_size
    summed_all = lax.psum(partial_value, "rep")
    summed_own = lax.dynamic_slice_in_dim(summed_all, rep_index * own_rows, own_rows, 0)
    aggregated = summed_own.astype(jnp.bfloat16)
    pre = jnp.dot(aggregated, weight, preferred_element_type=jnp.float32) + bias
    hidden = jax.nn.silu(pre).astype(jnp.bfloat16)
    sigmoid_pre = jax.nn.sigmoid(pre)
    slope = (
        cotangent.astype(jnp.float32) * (sigmoid_pre * (1.0 + pre * (1.0 - sigmoid_pre)))
    ).astype(jnp.bfloat16)
    local_weight = jnp.einsum("nd,nf->df", aggregated, slope, preferred_element_type=jnp.float32)
    local_bias = jnp.sum(slope.astype(jnp.float32), axis=0)
    weight_sum, bias_sum = lax.psum((local_weight, local_bias), ("section", "rep"))
    node_total = lax.axis_size("section") * rep_count * own_rows
    factor = 1.0 / math.sqrt(node_total)
    return (hidden, weight_sum * factor, bias_sum * factor)


def solution(mesh):
    in_specs = (
        P(("section", "rep"), None),
        P("section", "rep", None),
        P("section", "rep"),
        P("section", "rep", None, None, None),
        P(),
        P(),
        P(("section", "rep"), None),
    )
    out_specs = (P(("section", "rep"), None), P(), P())
    return jax.shard_map(shards, mesh=mesh, in_specs=in_specs, out_specs=out_specs, check_vma=False)
```

profile of v0, /device:TPU:24, one launch (start us, length us, event | category | flops | bytes accessed | tf_op | source)
XLA Modules:
  0.0 583.3 jit_solution(16949796323749232449)
XLA Ops:
  7.2 0.7 all-gather.2.cloned.1.call-update
  8.0 1.3 reduce_max.9
  9.9 0.7 iota_compare_fusion
  10.7 0.7 add_select_fusion
  11.4 185.0 %all-gather.2.cloned.1.call-done = bf16[8192,512]{1,0:T(8,128)(2,1)} async-done(((bf16[128,512]{1,0:T(8,128)(2,1)}), bf16[8192,512]{1,0:T(8,128)(2,1)}) %all-gather.2.cloned.1.call-update) | async-done | bytes 8388624 | tf_op jit(solution)/shard_map/all_gather | solution.py:22
  196.4 0.2 broadcast_in_dim.21
  196.7 30.3 %while.10 = (s32[]{:T(128)}, f32[8,128,512]{2,1,0:T(8,128)S(1)}, s32[]{:T(128)}, pred[8,12]{1,0:T(8,128)(4,1)S(1)}, bf16[8,12,128,128]{3,2,1,0:T(8,128)(2,1)}, /...) while((s32[]{:T(128)}, f32[8,128,512]{2,1,0:T(8,128)S(1)}, ...), condition=%wide.region_2.3_spmd, body=%wide.region_1.2_spmd.sunk | while | flops 537920640 | bytes 17830920 | solution.py:38
  196.7 0.1 compare_select_fusion.2
  196.8 0.1 reshape.32
  196.8 6.2 %gather_fusion = bf16[32,128,512]{2,1,0:T(8,128)(2,1)} fusion(bf16[64,128,512]{2,1,0:T(8,128)(2,1)} %get-tuple-element.131, s32[1024]{0:T(1024)S(1)} %pad_clamp_fusion.2), kind=kCustom, calls=%fused_computation.clone.1 | custom fusion | bytes 8388736 | tf_op jit(solution)/shard_map/while/body/gather | solution.py:33
  203.1 3.6 bitcast_add_fusion.2
  206.8 0.1 reshape.32
  206.9 6.2 %gather_fusion = bf16[32,128,512]{2,1,0:T(8,128)(2,1)} fusion(bf16[64,128,512]{2,1,0:T(8,128)(2,1)} %get-tuple-element.131, s32[1024]{0:T(1024)S(1)} %pad_clamp_fusion.2), kind=kCustom, calls=%fused_computation.clone.1 | custom fusion | bytes 8388736 | tf_op jit(solution)/shard_map/while/body/gather | solution.py:33
  213.2 3.6 bitcast_add_fusion.2
  216.9 0.1 reshape.32
  217.0 6.2 %gather_fusion = bf16[32,128,512]{2,1,0:T(8,128)(2,1)} fusion(bf16[64,128,512]{2,1,0:T(8,128)(2,1)} %get-tuple-element.131, s32[1024]{0:T(1024)S(1)} %pad_clamp_fusion.2), kind=kCustom, calls=%fused_computation.clone.1 | custom fusion | bytes 8388736 | tf_op jit(solution)/shard_map/while/body/gather | solution.py:33
  223.3 3.6 bitcast_add_fusion.2
  227.0 67.9 %all-reduce.4 = bf16[1024,512]{1,0:T(8,128)(2,1)} all-reduce(f32[1024,512]{1,0:T(8,128)S(1)} %bitcast.19), channel_id=1, replica_groups=mesh['section'=64,'rep'=8] {'rep'}, use_global_device_ids=true, to_apply=%region_3.4 | all-reduce | flops 524288 | bytes 3145728 | tf_op jit(solution)/shard_map/psum | solution.py:41
  294.8 1.9 convert_reduce_fusion
  296.7 2.3 fusion.6
  299.0 99.1 %psum.23 = f32[512]{0:T(512)S(1)} all-reduce(f32[512]{0:T(512)S(1)} %get-tuple-element.56), channel_id=1, replica_groups=mesh['section'=64,'rep'=8] {'section','rep'}, use_global_device_ids=true, to_apply=%region_6.7 | all-reduce | flops 512 | bytes 4096 | tf_op jit(solution)/shard_map/psum | solution.py:52
  398.1 0.6 broadcast_multiply_fusion.1
  398.7 175.6 %all-reduce.3.cloned.1.call-done = f32[512,512]{1,0:T(8,128)} async-done(((f32[512,512]{1,0:T(8,128)}), f32[512,512]{1,0:T(8,128)}) %all-reduce.3.cloned.1.call-update) | async-done | bytes 1048592 | tf_op jit(solution)/shard_map/psum | solution.py:52
  574.2 2.3 broadcast_multiply_fusion
  (17 shorter events, 0.5 us)
Async XLA Ops:
  7.2 287.7 %copy-start = (bf16[512,512]{1,0:T(8,128)(2,1)S(1)}, bf16[512,512]{1,0:T(8,128)(2,1)}, u32[]{:S(2)}) copy-start(bf16[512,512]{1,0:T(8,128)(2,1)} %param.13) | copy-start | bytes 1572868
  7.2 189.2 %all-gather.2.cloned.1.call-start = ((), (), s32[]{:S(2)}) async-start(), calls=%async_computation | async-start | bytes 8519680 | tf_op jit(solution)/shard_map/all_gather | solution.py:22
  7.9 566.3 %all-reduce.3.cloned.1.call-start = ((), (), s32[]{:S(2)}) async-start(), calls=%async_computation.1 | async-start | bytes 2097152 | tf_op jit(solution)/shard_map/psum | solution.py:52
  226.9 67.9 %copy-start.1 = (bf16[128,512]{1,0:T(8,128)(2,1)S(1)}, bf16[128,512]{1,0:T(8,128)(2,1)}, u32[]{:S(2)}) copy-start(bf16[128,512]{1,0:T(8,128)(2,1)} %param.15) | copy-start | bytes 393220
  226.9 67.9 %copy-start.2 = (f32[512]{0:T(512)S(1)}, f32[512]{0:T(512)}, u32[]{:S(2)}) copy-start(f32[512]{0:T(512)} %param.14) | copy-start | bytes 6148
Sparse Core Ops, SparseCore 0:
  12.3 183.9 all-gather.1
  299.1 275.0 all-reduce.2
where the time goes:
time: 584 us; the launch traced here: 583 us
  waiting for transfers between devices  361 us (62%)
  blocking collectives  167 us (29%)
  local copies, waits for them, and re-layouts  19.3 us (3%)
  matrix products  15.1 us (3%)
  between operations  14.8 us (3%)
  other arithmetic  5.84 us (1%)
    all_gather x1, waiting for transfers between devices, shards(): gathered = lax.all_gather(features, 'section', axis=0, tiled=True)  185 us
    psum x1, waiting for transfers between devices, shards(): lax.psum((local_weight, local_bias), ('section', 'rep'))  176 us
    psum x1, blocking collectives, shards(): lax.psum((local_weight, local_bias), ('section', 'rep'))  99.1 us
    psum x1, blocking collectives, shards(): summed_all = lax.psum(partial_value, 'rep')  67.9 us
    gather x3, local copies, waits for them, and re-layouts, one_turn(): picked = all_panels[step_cols]  18.5 us
  transfers between devices with their start and end apart: 2, of which 2 were waited for; matrix products, arithmetic and copies ran while one was open for 1% of the time, Pallas kernels for 0%

commit v1 on v0

--- a/solution.py
+++ b/solution.py
@@ -3,6 +3,7 @@
 import jax.numpy as jnp
 from jax import lax
 from jax.sharding import PartitionSpec as P
+from jax.lax import all_to_all, axis_size
 
 
 def shards(features, col_panels, block_counts, block_values, weight, bias, cotangent):
@@ -19,7 +20,10 @@
     slot_mask = jnp.arange(slot_count, dtype=jnp.int32)[None, :] < live_counts[:, None]
     tiles = block_values[:, 0]
     empty = jnp.zeros((row_panels, tile_size, feat_width), jnp.float32)
-    gathered = lax.all_gather(features, "section", axis=0, tiled=True)
+    gathered = jnp.concatenate(
+        all_to_all(jnp.stack([features for _ in range(axis_size("section"))], 0), "section", 0, 0),
+        0,
+    )
     all_panels = gathered.reshape(-1, tile_size, feat_width)
     slot_step = 4
     turn_count = (jnp.max(live_counts) + slot_step - 1) // slot_step

time: 584 us -> 656 us (1.12)
  waiting for transfers between devices: 361 us -> 412 us
  starting transfers between devices: 0.08 us -> 16.8 us
    all_to_all x0 -> x1, waiting for transfers between devices: none -> 237 us  [shards(): all_to_all(jnp.stack([features for _ in range(axis_size('section'))], 0),...]
    all_gather x1 -> x0, waiting for transfers between devices: 185 us -> none  [shards(): gathered = lax.all_gather(features, 'section', axis=0, tiled=True)]
    all_to_all x0 -> x1, starting transfers between devices: none -> 16.7 us  [shards(): all_to_all(jnp.stack([features for _ in range(axis_size('section'))], 0),...]
    psum x1, blocking collectives: 99.1 us -> 110 us  [shards(): lax.psum((local_weight, local_bias), ('section', 'rep'))]
    psum x1, blocking collectives: 67.9 us -> 58.5 us  [shards(): summed_all = lax.psum(partial_value, 'rep')]
  transfers between devices with their start and end apart: 2 -> 2, of which waited for: 2 -> 2; matrix products, arithmetic and copies ran while one was open for 1% -> 0% of each run, Pallas kernels for 0% -> 0%
where the time goes in v1:
time: 656 us
  waiting for transfers between devices  412 us (63%)
  blocking collectives  168 us (26%)
  local copies, waits for them, and re-layouts  24.4 us (4%)
  starting transfers between devices  16.8 us (3%)
  matrix products  15.1 us (2%)
  between operations  14.8 us (2%)
    all_to_all x1, waiting for transfers between devices, shards(): all_to_all(jnp.stack([features for _ in range(axis_size('section'))], 0),...  237 us
    psum x1, waiting for transfers between devices, shards(): lax.psum((local_weight, local_bias), ('section', 'rep'))  176 us
    psum x1, blocking collectives, shards(): lax.psum((local_weight, local_bias), ('section', 'rep'))  110 us
    psum x1, blocking collectives, shards(): summed_all = lax.psum(partial_value, 'rep')  58.5 us
    gather x3, local copies, waits for them, and re-layouts, one_turn(): picked = all_panels[step_cols]  18.5 us
    all_to_all x1, starting transfers between devices, shards(): all_to_all(jnp.stack([features for _ in range(axis_size('section'))], 0),...  16.7 us
  transfers between devices with their start and end apart: 2, of which 2 were waited for; matrix products, arithmetic and copies ran while one was open for 0% of the time, Pallas kernels for 0%

profile of v1, /device:TPU:24, one launch (start us, length us, event | category | flops | bytes accessed | tf_op | source)
XLA Modules:
  0.0 655.7 jit_solution(6080406406406567068)
XLA Ops:
  7.2 5.2 stack.2
  12.4 16.7 %all-to-all-start = ((bf16[64,128,512]{2,1,0:T(8,128)(2,1)}), bf16[64,128,512]{2,1,0:T(8,128)(2,1)}, u32[]{:S(2)}, u32[]{:S(2)}) async-start(bf16[64,128,512]{2,1,0:T(8,128)(2,1)} %stack.2), calls=%async_computation | async-start | bytes 16777216 | tf_op jit(solution)/shard_map/all_to_all | solution.py:24
  29.2 0.6 reduce_max.9
  30.6 236.6 %all-to-all-done = bf16[64,128,512]{2,1,0:T(8,128)(2,1)} async-done(((bf16[64,128,512]{2,1,0:T(8,128)(2,1)}), bf16[64,128,512]{2,1,0:T(8,128)(2,1)}, u32[]{:S(2)}, u32[]{:S(2)}) %all-to-all-start) | async-done | bytes 8388640 | tf_op jit(solution)/shard_map/all_to_all | solution.py:24
  267.2 0.2 broadcast_in_dim.21
  267.4 30.3 %while.10 = (s32[]{:T(128)}, f32[8,128,512]{2,1,0:T(8,128)S(1)}, s32[]{:T(128)}, pred[8,12]{1,0:T(8,128)(4,1)S(1)}, bf16[8,12,128,128]{3,2,1,0:T(8,128)(2,1)}, /...) while((s32[]{:T(128)}, f32[8,128,512]{2,1,0:T(8,128)S(1)}, ...), condition=%wide.region_2.3_spmd, body=%wide.region_1.2_spmd.sunk | while | flops 537920640 | bytes 17830920 | solution.py:42
  267.5 0.1 compare_select_fusion.2
  267.5 0.1 reshape.30
  267.6 6.2 gather_fusion
  273.9 3.6 bitcast_add_fusion.2
  277.6 0.1 compare_select_fusion.2
  277.6 0.1 reshape.30
  277.7 6.2 gather_fusion
  284.0 3.6 bitcast_add_fusion.2
  287.7 0.1 reshape.30
  287.8 6.2 gather_fusion
  294.1 3.6 bitcast_add_fusion.2
  297.7 58.5 %all-reduce.4 = bf16[1024,512]{1,0:T(8,128)(2,1)} all-reduce(f32[1024,512]{1,0:T(8,128)S(1)} %bitcast.18), channel_id=1, replica_groups=mesh['section'=64,'rep'=8] {'rep'}, use_global_device_ids=true, to_apply=%region_3.4 | all-reduce | flops 524288 | bytes 3145728 | tf_op jit(solution)/shard_map/psum | solution.py:45
  356.3 1.9 convert_reduce_fusion
  358.2 2.3 fusion.6
  360.5 109.9 %psum.23 = f32[512]{0:T(512)S(1)} all-reduce(f32[512]{0:T(512)S(1)} %get-tuple-element.56), channel_id=1, replica_groups=mesh['section'=64,'rep'=8] {'section','rep'}, use_global_device_ids=true, to_apply=%region_6.7 | all-reduce | flops 512 | bytes 4096 | tf_op jit(solution)/shard_map/psum | solution.py:56
  470.4 0.6 broadcast_multiply_fusion.1
  471.0 175.6 %all-reduce.3.cloned.1.call-done = f32[512,512]{1,0:T(8,128)} async-done(((f32[512,512]{1,0:T(8,128)}), f32[512,512]{1,0:T(8,128)}) %all-reduce.3.cloned.1.call-update) | async-done | bytes 1048592 | tf_op jit(solution)/shard_map/psum | solution.py:56
  646.5 2.3 broadcast_multiply_fusion
  (21 shorter events, 0.5 us)
Async XLA Ops:
  7.2 349.1 %copy-start = (bf16[512,512]{1,0:T(8,128)(2,1)S(1)}, bf16[512,512]{1,0:T(8,128)(2,1)}, u32[]{:S(2)}) copy-start(bf16[512,512]{1,0:T(8,128)(2,1)} %param.13) | copy-start | bytes 1572868
  12.4 16.8 %copy-start.4 = (s32[8,1]{0,1:T(1,128)S(1)}, s32[8,1]{0,1:T(1,128)}, u32[]{:S(2)}) copy-start(s32[8,1]{0,1:T(1,128)} %param.11) | copy-start | bytes 100
  12.4 18.2 %copy-start.1 = (s32[8,1,12]{2,1,0:T(1,128)S(1)}, s32[8,1,12]{2,1,0:T(1,128)}, u32[]{:S(2)}) copy-start(s32[8,1,12]{2,1,0:T(1,128)} %param.10) | copy-start | bytes 1156
  12.4 254.8 %all-to-all-start = ((bf16[64,128,512]{2,1,0:T(8,128)(2,1)}), bf16[64,128,512]{2,1,0:T(8,128)(2,1)}, u32[]{:S(2)}, u32[]{:S(2)}) async-start(bf16[64,128,512]{2,1,0:T(8,128)(2,1)} %stack.2), calls=%async_computation | async-start | bytes 16777216 | tf_op jit(solution)/shard_map/all_to_all | solution.py:24
  29.1 617.4 %all-reduce.3.cloned.1.call-start = ((), (), s32[]{:S(2)}) async-start(), calls=%async_computation.1 | async-start | bytes 2097152 | tf_op jit(solution)/shard_map/psum | solution.py:56
  297.7 58.6 %copy-start.2 = (bf16[128,512]{1,0:T(8,128)(2,1)S(1)}, bf16[128,512]{1,0:T(8,128)(2,1)}, u32[]{:S(2)}) copy-start(bf16[128,512]{1,0:T(8,128)(2,1)} %param.15) | copy-start | bytes 393220
  297.7 58.6 %copy-start.3 = (f32[512]{0:T(512)S(1)}, f32[512]{0:T(512)}, u32[]{:S(2)}) copy-start(f32[512]{0:T(512)} %param.14) | copy-start | bytes 6148
Sparse Core Ops, SparseCore 0:
  360.6 285.8 all-reduce.2

commit v2 on v0

--- a/solution.py
+++ b/solution.py
@@ -6,6 +6,10 @@
 
 
 def shards(features, col_panels, block_counts, block_values, weight, bias, cotangent):
+
+    def sizes_name(payload):
+        return jnp.sum(lax.all_gather(payload, "rep"), axis=0)
+
     rep_count = lax.axis_size("rep")
     rep_index = lax.axis_index("rep")
     tile_size = block_values.shape[-1]
@@ -38,7 +42,7 @@
     gathered_sum = lax.fori_loop(0, turn_count, one_turn, empty)
     partial_value = gathered_sum.reshape(row_panels * tile_size, feat_width)
     own_rows = own_panels * tile_size
-    summed_all = lax.psum(partial_value, "rep")
+    summed_all = sizes_name(partial_value)
     summed_own = lax.dynamic_slice_in_dim(summed_all, rep_index * own_rows, own_rows, 0)
     aggregated = summed_own.astype(jnp.bfloat16)
     pre = jnp.dot(aggregated, weight, preferred_element_type=jnp.float32) + bias

time: 584 us -> 703 us (1.20)
  waiting for transfers between devices: 361 us -> 540 us
  blocking collectives: 167 us -> 101 us
  other arithmetic: 5.84 us -> 13.9 us
    all_gather x0 -> x1, waiting for transfers between devices: none -> 177 us  [sizes_name(): return jnp.sum(lax.all_gather(payload, 'rep'), axis=0)]
    psum x1 -> x0, blocking collectives: 67.9 us -> none  [shards(): summed_all = lax.psum(partial_value, 'rep')]
    reduce_sum x0 -> x1, other arithmetic: none -> 8.09 us  [sizes_name(): return jnp.sum(lax.all_gather(payload, 'rep'), axis=0)]
  transfers between devices with their start and end apart: 2 -> 3, of which waited for: 2 -> 3; matrix products, arithmetic and copies ran while one was open for 1% -> 0% of each run, Pallas kernels for 0% -> 0%
where the time goes in v2:
time: 703 us
  waiting for transfers between devices  540 us (77%)
  blocking collectives  101 us (14%)
  local copies, waits for them, and re-layouts  20.6 us (3%)
  between operations  14.5 us (2%)
  other arithmetic  13.9 us (2%)
  matrix products  13.2 us (2%)
    all_gather x1, waiting for transfers between devices, shards(): gathered = lax.all_gather(features, 'section', axis=0, tiled=True)  185 us
    psum x1, waiting for transfers between devices, shards(): lax.psum((local_weight, local_bias), ('section', 'rep'))  177 us
    all_gather x1, waiting for transfers between devices, sizes_name(): return jnp.sum(lax.all_gather(payload, 'rep'), axis=0)  177 us
    psum x1, blocking collectives, shards(): lax.psum((local_weight, local_bias), ('section', 'rep'))  101 us
    gather x3, local copies, waits for them, and re-layouts, one_turn(): picked = all_panels[step_cols]  18.5 us
  transfers between devices with their start and end apart: 3, of which 3 were waited for; matrix products, arithmetic and copies ran while one was open for 0% of the time, Pallas kernels for 0%

profile of v2, /device:TPU:24, one launch (start us, length us, event | category | flops | bytes accessed | tf_op | source)
XLA Modules:
  0.0 702.6 jit_solution(7923130414993340645)
XLA Ops:
  7.2 0.7 all-gather.3.cloned.1.call-update
  8.0 1.3 reduce_max.9
  9.9 0.7 iota_compare_fusion
  10.7 0.7 add_select_fusion
  11.4 185.0 %all-gather.3.cloned.1.call-done = bf16[8192,512]{1,0:T(8,128)(2,1)} async-done(((bf16[128,512]{1,0:T(8,128)(2,1)}), bf16[8192,512]{1,0:T(8,128)(2,1)}) %all-gather.3.cloned.1.call-update) | async-done | bytes 8388624 | tf_op jit(solution)/shard_map/all_gather | solution.py:26
  196.4 0.2 broadcast_in_dim.21
  196.7 30.3 %while.10 = (s32[]{:T(128)}, f32[8,128,512]{2,1,0:T(8,128)S(1)}, s32[]{:T(128)}, pred[8,12]{1,0:T(8,128)(4,1)S(1)}, bf16[8,12,128,128]{3,2,1,0:T(8,128)(2,1)}, /...) while((s32[]{:T(128)}, f32[8,128,512]{2,1,0:T(8,128)S(1)}, ...), condition=%wide.region_2.3_spmd, body=%wide.region_1.2_spmd.sunk | while | flops 537920640 | bytes 17830920 | solution.py:42
  196.8 0.1 reshape.28
  196.9 6.2 gather_fusion
  203.1 3.6 bitcast_add_fusion.2
  206.9 0.1 reshape.28
  206.9 6.2 gather_fusion
  213.2 3.6 bitcast_add_fusion.2
  217.0 6.2 gather_fusion
  223.3 3.7 bitcast_add_fusion.2
  227.0 1.3 copy-done.1
  228.4 176.7 %all-gather.5.cloned.1.call-done = f32[8,1024,512]{2,1,0:T(8,128)} async-done(((f32[1,1024,512]{2,1,0:T(8,128)}), f32[8,1024,512]{2,1,0:T(8,128)}) %all-gather.5.cloned.1.call-update) | async-done | bytes 16777232 | tf_op jit(solution)/shard_map/all_gather | solution.py:11
  405.1 8.1 %reduce_sum.18 = bf16[1024,512]{1,0:T(8,128)(2,1)S(1)} reduce(f32[8,1024,512]{2,1,0:T(8,128)} %all-gather.5.cloned.1.call-done, f32[]{:T(128)} %constant.65.clone.1), dimensions={0}, to_apply=%region_3.4 | reduce | flops 3670016 | bytes 17825796 | tf_op jit(solution)/shard_map/reduce_sum | solution.py:11
  413.2 1.0 convert_reduce_fusion
  414.2 1.3 fusion.6
  415.5 100.6 %psum.15 = f32[512]{0:T(512)S(1)} all-reduce(f32[512]{0:T(512)S(1)} %get-tuple-element.56), channel_id=1, replica_groups=mesh['section'=64,'rep'=8] {'section','rep'}, use_global_device_ids=true, to_apply=%region_6.7 | all-reduce | flops 512 | bytes 4096 | tf_op jit(solution)/shard_map/psum | solution.py:56
  516.1 0.6 broadcast_multiply_fusion.1
  516.6 177.1 %all-reduce.2.cloned.1.call-done = f32[512,512]{1,0:T(8,128)} async-done(((f32[512,512]{1,0:T(8,128)}), f32[512,512]{1,0:T(8,128)}) %all-reduce.2.cloned.1.call-update) | async-done | bytes 1048592 | tf_op jit(solution)/shard_map/psum | solution.py:56
  693.7 2.3 broadcast_multiply_fusion
  (22 shorter events, 0.7 us)
Async XLA Ops:
  7.2 406.0 %copy-start = (bf16[512,512]{1,0:T(8,128)(2,1)S(1)}, bf16[512,512]{1,0:T(8,128)(2,1)}, u32[]{:S(2)}) copy-start(bf16[512,512]{1,0:T(8,128)(2,1)} %param.13) | copy-start | bytes 1572868
  7.2 189.2 %all-gather.3.cloned.1.call-start = ((), (), s32[]{:S(2)}) async-start(), calls=%async_computation | async-start | bytes 8519680 | tf_op jit(solution)/shard_map/all_gather | solution.py:26
  7.9 397.1 %all-gather.5.cloned.1.call-start = ((), (), s32[]{:S(2)}) async-start(), calls=%async_computation.1 | async-start | bytes 18874368 | tf_op jit(solution)/shard_map/all_gather | solution.py:11
  227.0 1.3 copy-start.1
  228.3 465.4 %all-reduce.2.cloned.1.call-start = ((), (), s32[]{:S(2)}) async-start(), calls=%async_computation.2 | async-start | bytes 2097152 | tf_op jit(solution)/shard_map/psum | solution.py:56
  228.4 184.8 %copy-start.2 = (bf16[128,512]{1,0:T(8,128)(2,1)S(1)}, bf16[128,512]{1,0:T(8,128)(2,1)}, u32[]{:S(2)}) copy-start(bf16[128,512]{1,0:T(8,128)(2,1)} %param.15) | copy-start | bytes 393220
  228.4 184.8 %copy-start.3 = (f32[512]{0:T(512)S(1)}, f32[512]{0:T(512)}, u32[]{:S(2)}) copy-start(f32[512]{0:T(512)} %param.14) | copy-start | bytes 6148
Sparse Core Ops, SparseCore 0:
  12.3 184.0 all-gather.2
  228.4 176.5 all-gather.4
  415.6 278.0 all-reduce.1
